TPU v7x, 32 devices: a whole 2x2x4 slice. The times are simulated.
32 devices in a mesh: groups: 2 (over x), seq: 16 (over z, y, core).
Axes of the slice: x: 2, y: 2, z: 4, core: 2. Of those that a mesh axis runs over, the one named last changes fastest.
Arguments:
- query: bfloat16 [4096, 1024], P(('groups', 'seq')), parts along dimension 0, as said below
- keys: bfloat16 [4096, 1024], P(('groups', 'seq')), parts along dimension 0, as said below
- values: bfloat16 [4096, 1024], P(('groups', 'seq')), parts along dimension 0, may hold values from -6 to 6
- out_weight: bfloat16 [1024, 2048], P('seq'), may hold values from -0.1875 to 0.1875
- grad_out: bfloat16 [4096, 2048], P(('groups', 'seq')), parts along dimension 0, may hold values from -6 to 6
- global_blocks: int32 [4], P('groups'), parts along dimension 0, may hold values from 0 to 15
- random_blocks: int32 [32, 3], P(('groups', 'seq')), parts along dimension 0, may hold values from 0 to 15, as said below
Outputs:
- layer_out: bfloat16 [4096, 2048], P(('groups', 'seq')), parts along dimension 0
- grad_query: bfloat16 [4096, 1024], P(('groups', 'seq')), parts along dimension 0
- grad_keys: bfloat16 [4096, 1024], P(('groups', 'seq')), parts along dimension 0
- grad_values: bfloat16 [4096, 1024], P(('groups', 'seq')), parts along dimension 0
- grad_weight: float32 [2048, 2048], P(('groups', 'seq')), parts along dimension 0
There are 2 independent parts, one for each index of `groups`. A program takes and returns all parts, laid end to end along the dimension named above; an argument that names none is the same for every part. Nothing has to cross between parts.
Inputs may be any that keep to these rules, and one draw needn't show every extreme that they name: `random_blocks`: random block r of query block b lies on the device that holds b or on a device beside it: it is at least max(b - 1, 0) * 1 and below min(b + 2, 16). `query`: entries lie between -12 and 12. `keys`: entries lie between -6 and 6.
All inputs are finite; a program needn't handle non-finite values.
Results may differ from a plain program's by a relative error of at most 0.012.
Values may be sent and summed in bfloat16 or wider, within the bound.
No kernel may reach another device: no remote copies, remote signals or barrier semaphores. Data moves between devices by JAX's collectives and lax.ppermute only.
A program may use at most 128 MiB of HBM per device.

v0:
```python
import math
import jax
import jax.numpy as jnp
from jax import lax
from jax.sharding import PartitionSpec as P

H = 8
BLK = 128
NEG_FILL = -1e30


def extended_2(shard, sides, width):
    for axis, dim in sides:
        count, length = (lax.axis_size(axis), shard.shape[dim])
        up = [(i, (i + 1) % count) for i in range(count - 1)]
        down = [(j, i) for i, j in up]
        last = lax.slice_in_dim(shard, length - width, length, axis=dim)
        initial = lax.slice_in_dim(shard, 0, width, axis=dim)
        before = lax.ppermute(last, axis, up)
        after = lax.ppermute(initial, axis, down)
        shard = jnp.concatenate([before, shard, after], axis=dim)
    return shard


def spread(shard, axis, root):
    mine = lax.axis_index(axis) == root
    return lax.psum(jnp.where(mine, shard, jnp.zeros_like(shard)), axis)


def window_and_random(random_rows, device, blocks_dev, total_blocks):
    local_ids = jnp.arange(blocks_dev, dtype=jnp.int32)
    global_ids = device * blocks_dev + local_ids
    offsets = jnp.array([-1, 0, 1], dtype=jnp.int32)
    neighbour_ids = global_ids[:, None] + offsets[None, :]
    window_index = local_ids[:, None] + blocks_dev + offsets[None, :]
    window_live = (neighbour_ids >= 0) & (neighbour_ids < total_blocks)
    random_index = random_rows - (device - 1) * blocks_dev
    ext_index = jnp.concatenate([window_index, random_index], axis=1)
    live_local = jnp.concatenate(
        [window_live, jnp.ones(random_rows.shape, dtype=jnp.bool_)], axis=1
    )
    return (ext_index, live_local)


def choose_blocks(extended, global_kv, ext_index, live_local, blocks_dev):
    feature_count = extended.shape[2]
    ext_blocks = extended.reshape(2, 3 * blocks_dev, BLK, feature_count)
    local_sel = jnp.take(ext_blocks, ext_index, axis=1)
    global_count = global_kv.shape[0]
    global_sel = jnp.swapaxes(global_kv, 0, 1)[:, None]
    chosen = jnp.concatenate([local_sel, global_sel], axis=2)
    listed = chosen.shape[2]
    chosen = chosen.reshape(2, blocks_dev, listed * BLK, H, feature_count // H)
    live = jnp.concatenate(
        [live_local, jnp.ones((blocks_dev, global_count), dtype=jnp.bool_)], axis=1
    )
    live_rows = jnp.repeat(live, BLK, axis=1)
    return (chosen[0], chosen[1], live_rows)


def attend_blocks(query_blocks, chosen_keys, chosen_values, live_rows):
    score_scale = 1.0 / math.sqrt(query_blocks.shape[-1])
    scores = (
        jnp.einsum("qihd,qjhd->qhij", query_blocks, chosen_keys, preferred_element_type=jnp.float32)
        * score_scale
    )
    scores = jnp.where(live_rows[:, None, None, :], scores, NEG_FILL)
    row_top = jnp.max(scores, axis=-1, keepdims=True)
    raised = jnp.exp(scores - row_top)
    soft_weights = raised / jnp.sum(raised, axis=-1, keepdims=True)
    rounded_weights = soft_weights.astype(jnp.bfloat16)
    mixed_out = jnp.einsum(
        "qhij,qjhd->qihd", rounded_weights, chosen_values, preferred_element_type=jnp.float32
    )
    return (soft_weights, rounded_weights, mixed_out.astype(jnp.bfloat16))


def attend_backward(
    query_blocks, chosen_keys, chosen_values, soft_weights, rounded_weights, upstream_blocks
):
    score_scale = 1.0 / math.sqrt(query_blocks.shape[-1])
    grad_chosen_values = jnp.einsum(
        "qhij,qihd->qjhd", rounded_weights, upstream_blocks, preferred_element_type=jnp.float32
    )
    grad_weights = jnp.einsum(
        "qihd,qjhd->qhij", upstream_blocks, chosen_values, preferred_element_type=jnp.float32
    )
    row_delta = jnp.sum(soft_weights * grad_weights, axis=-1, keepdims=True)
    grad_scores = (score_scale * soft_weights * (grad_weights - row_delta)).astype(jnp.bfloat16)
    grad_query_blocks = jnp.einsum(
        "qhij,qjhd->qihd", grad_scores, chosen_keys, preferred_element_type=jnp.float32
    )
    grad_chosen_keys = jnp.einsum(
        "qhij,qihd->qjhd", grad_scores, query_blocks, preferred_element_type=jnp.float32
    )
    return (grad_query_blocks, grad_chosen_keys, grad_chosen_values)


def fold_gradients(grad_chosen_keys, grad_chosen_values, ext_index, blocks_dev):
    stacked = jnp.stack([grad_chosen_keys, grad_chosen_values])
    listed_local = ext_index.shape[1]
    feature_count = stacked.shape[3] * stacked.shape[4]
    stacked = stacked.reshape(2, blocks_dev, -1, BLK * feature_count)
    local_part = stacked[:, :, :listed_local].reshape(
        2, blocks_dev * listed_local, BLK * feature_count
    )
    one_hot = (
        ext_index.reshape(-1)[:, None] == jnp.arange(3 * blocks_dev, dtype=jnp.int32)[None, :]
    ).astype(jnp.float32)
    grad_ext = jnp.einsum("sj,ksx->kjx", one_hot, local_part, precision=lax.Precision.HIGHEST)
    grad_ext = grad_ext.reshape(2, 3 * blocks_dev * BLK, feature_count)
    grad_global = jnp.sum(stacked[:, :, listed_local:], axis=1).reshape(2, -1, BLK, feature_count)
    return (grad_ext, grad_global)


def local(query, keys, values, out_weight, grad_out, global_blocks, random_blocks):
    tok_rows = query.shape[0]
    feature_count = query.shape[1]
    blocks_dev = tok_rows // BLK
    device = lax.axis_index("seq")
    total_blocks = blocks_dev * lax.axis_size("seq")
    paired = jnp.stack([keys, values])
    extended = extended_2(paired, (("seq", 1),), tok_rows)
    fetched = []
    for global_slot in range(global_blocks.shape[0]):
        block_id = global_blocks[global_slot]
        owner_index = block_id // blocks_dev
        fetched.append(spread(paired, "seq", owner_index))
    global_kv = jnp.stack(fetched)
    ext_index, live_local = window_and_random(random_blocks, device, blocks_dev, total_blocks)
    chosen_keys, chosen_values, live_rows = choose_blocks(
        extended, global_kv, ext_index, live_local, blocks_dev
    )
    query_blocks = query.reshape(blocks_dev, BLK, H, feature_count // H)
    soft_weights, rounded_weights, mixed_out = attend_blocks(
        query_blocks, chosen_keys, chosen_values, live_rows
    )
    attn_out = mixed_out.reshape(tok_rows, feature_count)
    columns = attn_out
    layer_sum = jnp.dot(
        columns,
        lax.all_gather(out_weight, "seq", axis=0, tiled=True),
        preferred_element_type=jnp.float32,
    )
    upstream_sum = lax.dot_general(
        grad_out,
        lax.all_gather(out_weight, "seq", axis=0, tiled=True),
        (((1,), (1,)), ((), ())),
        preferred_element_type=jnp.float32,
    )
    layer_out = layer_sum.astype(jnp.bfloat16)
    upstream_blocks = upstream_sum.astype(jnp.bfloat16).reshape(
        blocks_dev, BLK, H, feature_count // H
    )
    columns = attn_out
    grad_weight = lax.psum_scatter(
        lax.dot_general(
            columns, grad_out, (((0,), (0,)), ((), ())), preferred_element_type=jnp.float32
        ),
        "seq",
        scatter_dimension=0,
        tiled=True,
    )
    grad_query_blocks, grad_chosen_keys, grad_chosen_values = attend_backward(
        query_blocks, chosen_keys, chosen_values, soft_weights, rounded_weights, upstream_blocks
    )
    grad_ext, grad_global = fold_gradients(
        grad_chosen_keys, grad_chosen_values, ext_index, blocks_dev
    )
    rim_grads = jnp.concatenate(
        [grad_ext[:, :tok_rows], grad_ext[:, 2 * tok_rows :]], axis=1
    ).astype(jnp.bfloat16)
    arrived = extended_2(rim_grads, (("seq", 1),), tok_rows)
    global_total = lax.psum(grad_global, "seq")
    owned_mask = (
        global_blocks[:, None]
        == device * blocks_dev + jnp.arange(blocks_dev, dtype=jnp.int32)[None, :]
    ).astype(jnp.float32)
    owned_sum = jnp.einsum(
        "gj,kgx->kjx",
        owned_mask,
        global_total.reshape(2, owned_mask.shape[0], -1),
        precision=lax.Precision.HIGHEST,
    )
    grad_paired = grad_ext[:, tok_rows : 2 * tok_rows] + arrived[:, :tok_rows].astype(jnp.float32)
    grad_paired = grad_paired + arrived[:, 3 * tok_rows :].astype(jnp.float32)
    grad_paired = grad_paired + owned_sum.reshape(2, tok_rows, feature_count)
    grad_paired = grad_paired.astype(jnp.bfloat16)
    grad_query = grad_query_blocks.reshape(tok_rows, feature_count).astype(jnp.bfloat16)
    return (layer_out, grad_query, grad_paired[0], grad_paired[1], grad_weight)


def solution(mesh):
    placed = (
        P(("groups", "seq"), None),
        P(("groups", "seq"), None),
        P(("groups", "seq"), None),
        P("seq", None),
        P(("groups", "seq"), None),
        P("groups"),
        P(("groups", "seq"), None),
    )
    return jax.shard_map(
        local,
        mesh=mesh,
        in_specs=placed,
        out_specs=(
            P(("groups", "seq"), None),
            P(("groups", "seq"), None),
            P(("groups", "seq"), None),
            P(("groups", "seq"), None),
            P(("groups", "seq"), None),
        ),
        check_vma=False,
    )
```

profile of v0, /device:TPU:0, one launch (start us, length us, event | category | flops | bytes accessed | tf_op | source)
XLA Modules:
  0.0 429.1 jit_solution(10546698557166395422)
XLA Ops:
  7.2 0.0 copy-start
  7.2 0.0 copy-start.12
  7.2 0.0 copy-start.11
  7.2 0.0 all-reduce.6.cloned.1.call-start
  7.3 1.4 fusion.36
  10.0 2.1 select_bitcast_fusion.1
  12.1 0.0 all-reduce.6.cloned.1.call-update
  12.1 0.0 all-gather.2.cloned.1.call-start
  12.1 0.7 all-gather.2.cloned.1.call-update
  12.8 0.0 all-reduce.4.cloned.1.call-start
  12.9 1.3 collective-permute-start.1
  14.2 3.8 collective-permute-start
  18.0 0.1 fusion.30
  18.1 0.1 compare_and_fusion
  18.2 0.1 fusion.28
  18.3 0.1 broadcast_bitcast_fusion
  18.4 0.5 collective-permute-done
  18.9 1.2 pad_maximum_fusion.2
  20.0 2.5 gather_fusion
  22.5 89.4 %all-reduce.6.cloned.1.call-done = (bf16[1,2,128,1024]{3,2,1,0:T(8,128)(2,1)}, bf16[1,2,128,1024]{3,2,1,0:T(8,128)(2,1)}) async-done(((bf16[1,2,128,1024]{3,2,1,0:T(8,128)(2,1)}, bf16[1,2,128,1024]{3,2,1,0:T(8,128)(2,1)}), (bf16[1,2,128,1024]{3,2,1,0:T(8,128)(2,1)}, bf16[1,2,128,1024]{3,2,1,0:T(8,128)(2,1)})) %all-reduce.6.cloned.1.call-update) | async-done | bytes 1048592 | tf_op jit(solution)/shard_map/psum | solution.py:27
  111.9 1.3 maximum_bitcast_fusion.2
  113.2 2.3 bitcast_select_fusion
  115.5 1.6 pad_maximum_fusion.1
  117.1 0.6 copy.57
  117.7 3.0 copy.52
  120.7 3.6 copy.58
  124.3 3.3 copy.34
  127.6 0.8 fusion.22
  128.4 3.4 fusion.37
  131.8 32.2 %all-gather.2.cloned.1.call-done = bf16[1024,2048]{1,0:T(8,128)(2,1)} async-done(((bf16[64,2048]{1,0:T(8,128)(2,1)}), bf16[1024,2048]{1,0:T(8,128)(2,1)}) %all-gather.2.cloned.1.call-update) | async-done | bytes 4194320 | tf_op jit(solution)/shard_map/all_gather | solution.py:142
  164.0 3.7 convolution_convert_fusion.3
  167.7 0.2 copy.55
  167.9 5.0 %convolution_bitcast_fusion.1 = f32[1,1024,8,128]{1,3,2,0:T(8,128)} fusion(bf16[128,8,128]{0,2,1:T(8,128)(2,1)S(1)} %bitcast.154, f32[8,128,1024]{1,2,0:T(8,128)} %get-tuple-element.29, f32[8,128]{1,0:T(8,128)S(1)} %get-tuple-element.28), kind=kOutput, calls=%fused_computation.19 | convolution fusion | flops 270532608 | bytes 8654848 | tf_op jit(solution)/shard_map/qhij,qihd->qjhd/dot_general | solution.py:82
  172.9 3.1 multiply_reduce_fusion
  176.0 5.4 %copy.40 = f32[1,1024,8,128]{3,2,1,0:T(8,128)} copy(f32[1,1024,8,128]{1,3,2,0:T(8,128)} %convolution_bitcast_fusion.1) | data formatting | bytes 8388608 | tf_op jit(solution)/shard_map/qhij,qihd->qjhd/transpose | solution.py:82
  181.3 4.9 %stack.34 = f32[1,1,8,131072]{3,2,1,0:T(8,128)} reshape(f32[1,1024,8,128]{3,2,1,0:T(8,128)} %copy.40) | data formatting | bytes 8388608 | tf_op jit(solution)/shard_map/stack | solution.py:100
  186.2 4.2 multiply_convert_fusion
  190.4 0.7 convolution_bitcast_fusion.2
  191.1 0.6 copy-done.1
  191.7 4.4 %copy.37 = f32[1,1024,8,128]{3,2,1,0:T(8,128)} copy(f32[1,1024,8,128]{3,1,2,0:T(8,128)S(1)} %convolution_bitcast_fusion.2) | data formatting | bytes 8388608 | tf_op jit(solution)/shard_map/qhij,qihd->qjhd/transpose | solution.py:93
  196.1 4.9 %stack.33 = f32[1,1,8,131072]{3,2,1,0:T(8,128)} reshape(f32[1,1024,8,128]{3,2,1,0:T(8,128)} %copy.37) | data formatting | bytes 8388608 | tf_op jit(solution)/shard_map/stack | solution.py:100
  201.0 5.7 %fusion.10 = f32[2,131072,2]{1,2,0:T(2,128)} fusion(f32[1,1,8,131072]{3,2,0,1:T(8,128)} %bitcast.138, f32[1,1,8,131072]{3,2,0,1:T(8,128)} %bitcast.140), kind=kLoop, calls=%fused_computation.23 | loop fusion | flops 524288 | bytes 10485760 | tf_op jit(solution)/shard_map/gj,kgx->kjx/dot_general | solution.py:179
  206.7 4.0 dot_general.56
  210.8 0.0 all-reduce.4.cloned.1.call-update
  210.8 0.3 reduce-scatter.2.cloned.1.call-start
  211.0 3.6 convolution_convert_fusion.2
  214.6 4.5 %fusion.38 = f32[1024,2048]{1,0:T(8,128)} fusion(bf16[128,1024]{0,1:T(8,128)(2,1)S(1)} %bitcast.147, bf16[128,2048]{1,0:T(8,128)(2,1)S(1)} %copy-done), kind=kOutput, calls=%fused_computation.75 | convolution fusion | flops 536870912 | bytes 9175040 | tf_op jit(solution)/shard_map/dot_general | solution.py:157
  219.1 0.0 reduce-scatter.2.cloned.1.call-update
  219.1 0.6 copy-done.10
  219.7 0.1 add_bitcast_fusion
  219.8 2.3 convolution_convert_fusion.1
  222.1 0.9 copy.43
  223.0 9.7 %convolution_bitcast_fusion = f32[2,3,131072]{2,1,0:T(4,128)} fusion(f32[1,1,8,131072]{3,2,0,1:T(8,128)} %bitcast.139, f32[1,1,8,131072]{3,2,0,1:T(8,128)} %bitcast.141, s32[6]{0:T(128)S(1)} %add_bitcast_fusion), kind=kOutput, calls=%fused_computation.2 | convolution fusion | flops 58195984 | bytes 11534360 | tf_op jit(solution)/shard_map/sj,ksx->kjx/dot_general | solution.py:110
  232.7 5.1 %reshape.362 = f32[2,384,1024]{2,1,0:T(8,128)} reshape(f32[2,3,131072]{2,1,0:T(4,128)} %convolution_bitcast_fusion) | data formatting | bytes 6291456 | tf_op jit(solution)/shard_map/reshape | solution.py:111
  237.8 2.3 convert.6
  240.1 0.1 fusion.35
  240.2 1.3 collective-permute-start.3
  241.5 3.3 collective-permute-start.2
  244.9 1.5 convolution_convert_fusion
  246.4 67.3 %all-reduce.4.cloned.1.call-done = f32[2,128,1024,2]{2,1,3,0:T(8,128)} async-done(((f32[2,128,1024,2]{2,1,3,0:T(8,128)}), f32[2,128,1024,2]{2,1,3,0:T(8,128)}) %all-reduce.4.cloned.1.call-update) | async-done | bytes 2097168 | tf_op jit(solution)/shard_map/psum | solution.py:174
  313.7 6.6 %fusion.13 = f32[1,2,128,1024]{3,0,2,1:T(1,128)S(1)} fusion(f32[2,128,1024,2]{2,1,3,0:T(8,128)} %all-reduce.4.cloned.1.call-done, s32[2]{0:T(128)S(1)} %copy-done.8, s32[]{:T(128)S(6)} %axis_index.8), kind=kOutput, calls=%fused_computation.28 | convolution fusion | flops 6291458 | bytes 3145740 | tf_op jit(solution)/shard_map/gj,kgx->kjx/dot_general | solution.py:179
  320.3 1.7 fusion.18
  322.0 0.8 slice_bitcast_fusion
  322.8 99.8 %reduce-scatter.2.cloned.1.call-done = f32[64,2048]{1,0:T(8,128)} async-done(((f32[1024,2048]{1,0:T(8,128)}), f32[64,2048]{1,0:T(8,128)}) %reduce-scatter.2.cloned.1.call-update) | async-done | bytes 524304 | tf_op jit(solution)/shard_map/reduce_scatter | solution.py:156
  (32 shorter events, 0.1 us)
Async XLA Ops:
  7.2 156.8 %copy-start = (bf16[128,2048]{1,0:T(8,128)(2,1)S(1)}, bf16[128,2048]{1,0:T(8,128)(2,1)}, u32[]{:S(2)}) copy-start(bf16[128,2048]{1,0:T(8,128)(2,1)} %param.12) | copy-start | bytes 1572868
  7.2 10.8 %copy-start.12 = (s32[1,3,1]{1,2,0:T(1,128)S(1)}, s32[1,3,1]{1,2,0:T(1,128)}, u32[]{:S(2)}) copy-start(s32[1,3,1]{1,2,0:T(1,128)} %constant.63) | copy-start | bytes 40
  7.2 10.9 %copy-start.11 = (s32[3]{0:T(128)S(1)}, s32[3]{0:T(128)}, u32[]{:S(2)}) copy-start(s32[3]{0:T(128)} %constant.60.clone) | copy-start | bytes 40
  7.2 11.7 %copy-start.6 = (bf16[128,1024]{1,0:T(8,128)(2,1)S(1)}, bf16[128,1024]{1,0:T(8,128)(2,1)}, u32[]{:S(2)}) copy-start(bf16[128,1024]{1,0:T(8,128)(2,1)} %param.10) | copy-start | bytes 786436
  7.2 11.7 %copy-start.7 = (bf16[128,1024]{1,0:T(8,128)(2,1)S(1)}, bf16[128,1024]{1,0:T(8,128)(2,1)}, u32[]{:S(2)}) copy-start(bf16[128,1024]{1,0:T(8,128)(2,1)} %param.9) | copy-start | bytes 786436
  7.2 10.8 %copy-start.9 = (s32[1,3]{1,0:T(1,128)S(1)}, s32[1,3]{1,0:T(1,128)}, u32[]{:S(2)}) copy-start(s32[1,3]{1,0:T(1,128)} %param.14) | copy-start | bytes 40
  7.2 104.7 %all-reduce.6.cloned.1.call-start = ((), (), s32[]{:S(2)}) async-start(), calls=%async_computation.4 | async-start | bytes 2097152 | tf_op jit(solution)/shard_map/psum | solution.py:27
  12.1 151.9 %all-gather.2.cloned.1.call-start = ((), (), s32[]{:S(2)}) async-start(), calls=%async_computation.1 | async-start | bytes 4456448 | tf_op jit(solution)/shard_map/all_gather | solution.py:142
  12.8 300.8 %all-reduce.4.cloned.1.call-start = ((), (), s32[]{:S(2)}) async-start(), calls=%async_computation.2 | async-start | bytes 4194304 | tf_op jit(solution)/shard_map/psum | solution.py:174
  12.9 5.5 %collective-permute-start.1 = (bf16[2,128,1024]{2,1,0:T(8,128)(2,1)S(1)}, bf16[2,128,1024]{2,1,0:T(8,128)(2,1)S(1)}, u32[]{:S(2)}, u32[]{:S(2)}) collective-permute-start(bf16[2,128,1024]{2,1,0:T(8,128)(2,1)S(1)} %get-tuple-element.25), channel_id=1, source_target_pairs={{1,0},{2,1},{3,2},{4,3},{5,4},{6,5},{7,6},{8,7},{9,8},{10,9},{11,1... | collective-permute-start | bytes 1572872 | tf_op jit(solution)/shard_map/ppermute | solution.py:20
  14.2 4.7 %collective-permute-start = (bf16[2,128,1024]{2,1,0:T(8,128)(2,1)S(1)}, bf16[2,128,1024]{2,1,0:T(8,128)(2,1)}, u32[]{:S(2)}, u32[]{:S(2)}) collective-permute-start(bf16[2,128,1024]{2,1,0:T(8,128)(2,1)S(1)} %get-tuple-element.25), channel_id=1, source_target_pairs={{0,1},{1,2},{2,3},{3,4},{4,5},{5,6},{6,7},{7,8},{8,9},{9,10},{10,1... | collective-permute-start | bytes 1572872 | tf_op jit(solution)/shard_map/ppermute | solution.py:19
  124.3 3.3 copy-start.5
  167.9 5.0 %copy-start.3 = (f32[8,128,1024]{1,2,0:T(8,128)S(1)}, f32[8,128,1024]{1,2,0:T(8,128)}, u32[]{:S(2)}) copy-start(f32[8,128,1024]{1,2,0:T(8,128)} %get-tuple-element.29) | copy-start | bytes 12582916
  167.9 5.0 %copy-start.4 = (bf16[1024,8,128]{0,2,1:T(8,128)(2,1)S(1)}, bf16[1024,8,128]{0,2,1:T(8,128)(2,1)}, u32[]{:S(2)}) copy-start(bf16[1024,8,128]{0,2,1:T(8,128)(2,1)} %copy.52) | copy-start | bytes 6291460
  190.4 1.4 copy-start.1
  210.8 211.8 %reduce-scatter.2.cloned.1.call-start = ((), (), s32[]{:S(2)}) async-start(), calls=%async_computation.3 | async-start | bytes 8912896 | tf_op jit(solution)/shard_map/reduce_scatter | solution.py:156
  219.1 0.7 copy-start.10
  237.8 7.0 %copy-start.2 = (bf16[1024,2048]{1,0:T(8,128)(2,1)S(1)}, bf16[1024,2048]{1,0:T(8,128)(2,1)}, u32[]{:S(2)}) copy-start(bf16[1024,2048]{1,0:T(8,128)(2,1)} %all-gather.2.cloned.1.call-done) | copy-start | bytes 12582916
  240.1 73.6 %copy-start.8 = (s32[2]{0:T(128)S(1)}, s32[2]{0:T(128)}, u32[]{:S(2)}) copy-start(s32[2]{0:T(128)} %param.13) | copy-start | bytes 28
  240.2 80.0 %collective-permute-start.3 = (bf16[2,128,1024]{2,1,0:T(8,128)(2,1)S(1)}, bf16[2,128,1024]{2,1,0:T(8,128)(2,1)S(1)}, u32[]{:S(2)}, u32[]{:S(2)}) collective-permute-start(bf16[2,128,1024]{2,1,0:T(8,128)(2,1)S(1)} %get-tuple-element.20), channel_id=1, source_target_pairs={{1,0},{2,1},{3,2},{4,3},{5,4},{6,5},{7,6},{8,7},{9,8},{10,9},{11,1... | collective-permute-start | bytes 1572872 | tf_op jit(solution)/shard_map/ppermute | solution.py:20
  241.5 78.8 %collective-permute-start.2 = (bf16[2,128,1024]{2,1,0:T(8,128)(2,1)S(1)}, bf16[2,128,1024]{2,1,0:T(8,128)(2,1)S(1)}, u32[]{:S(2)}, u32[]{:S(2)}) collective-permute-start(bf16[2,128,1024]{2,1,0:T(8,128)(2,1)S(1)} %get-tuple-element.19), channel_id=1, source_target_pairs={{0,1},{1,2},{2,3},{3,4},{4,5},{5,6},{6,7},{7,8},{8,9},{9,10},{10,1... | collective-permute-start | bytes 1572872 | tf_op jit(solution)/shard_map/ppermute | solution.py:19
Sparse Core Ops, SparseCore 0:
  12.2 99.7 all-reduce.5
  114.1 49.8 all-gather.1
  210.9 102.7 all-reduce.3
  318.7 103.8 reduce-scatter.1
where the time goes:
time: 430 us; the launch traced here: 429 us
  waiting for transfers between devices  290 us (67%)
  local copies, waits for them, and re-layouts  46.4 us (11%)
  matrix products  41.4 us (10%)
  other arithmetic  26 us (6%)
  between operations  15.3 us (4%)
  starting transfers between devices  10.1 us (2%)
    reduce_scatter x1, waiting for transfers between devices, local(): lax.psum_scatter(lax.dot_general(columns, grad_out, (((0,), (0,)), ((), (...  99.8 us
    psum x1, waiting for transfers between devices, spread(): return lax.psum(jnp.where(mine, shard, jnp.zeros_like(shard)), axis)  89.4 us
    psum x1, waiting for transfers between devices, local(): global_total = lax.psum(grad_global, 'seq')  67.3 us
    all_gather x1, waiting for transfers between devices, local(): lax.all_gather(out_weight, 'seq', axis=0, tiled=True)  32.2 us
    another operation x2, local copies, waits for them, and re-layouts, fold_gradients(): stacked = jnp.stack([grad_chosen_keys, grad_chosen_values])  9.74 us
    dot_general x1, matrix products, fold_gradients(): jnp.einsum('sj,ksx->kjx', one_hot, local_part, precision=lax.Precision.HI...  9.71 us
  transfers between devices with their start and end apart: 8, of which 5 were waited for; matrix products, arithmetic and copies ran while one was open for 15% of the time, Pallas kernels for 0%

commit v1 on v0

--- a/solution.py
+++ b/solution.py
@@ -7,6 +7,12 @@
 H = 8
 BLK = 128
 NEG_FILL = -1e30
+
+
+def gather_and_add(value, axis):
+    blocks = lax.all_gather(value, axis, axis=0, tiled=False)
+    total = blocks.sum(axis=0)
+    return total
 
 
 def extended_2(shard, sides, width):
@@ -171,7 +177,7 @@
         [grad_ext[:, :tok_rows], grad_ext[:, 2 * tok_rows :]], axis=1
     ).astype(jnp.bfloat16)
     arrived = extended_2(rim_grads, (("seq", 1),), tok_rows)
-    global_total = lax.psum(grad_global, "seq")
+    global_total = gather_and_add(grad_global, "seq")
     owned_mask = (
         global_blocks[:, None]
         == device * blocks_dev + jnp.arange(blocks_dev, dtype=jnp.int32)[None, :]

time: 430 us -> 506 us (1.18)
  waiting for transfers between devices: 290 us -> 346 us
  other arithmetic: 26 us -> 41.1 us
  local copies, waits for them, and re-layouts: 46.4 us -> 53.5 us
    all_gather x0 -> x1, waiting for transfers between devices: none -> 138 us  [gather_and_add(): blocks = lax.all_gather(value, axis, axis=0, tiled=False)]
    psum x1 -> x0, waiting for transfers between devices: 67.3 us -> none  [local(): global_total = lax.psum(grad_global, 'seq')]
    reduce_sum x0 -> x1, other arithmetic: none -> 12.1 us  [gather_and_add(): total = blocks.sum(axis=0)]
    reduce_scatter x1, waiting for transfers between devices: 99.8 us -> 89.4 us  [local(): lax.psum_scatter(lax.dot_general(columns, grad_out, (((0,), (0,)), ((), (...]
    dot_general x1 -> x0, other arithmetic: 5.72 us -> none  [local(): jnp.einsum('gj,kgx->kjx', owned_mask, global_total.reshape(2, owned_mask....]
    another operation x1 -> x2, other arithmetic: 2.31 us -> 7.96 us  [the longest x1 5.68 us: fold_gradients(): stacked = jnp.stack([grad_chosen_keys, grad_chosen_values])]
    another operation x5 -> x6, local copies, waits for them, and re-layouts: 6.49 us -> 11.6 us
  transfers between devices with their start and end apart: 8 -> 8, of which waited for: 5 -> 4; matrix products, arithmetic and copies ran while one was open for 15% -> 17% of each run, Pallas kernels for 0% -> 0%
where the time goes in v1:
time: 506 us
  waiting for transfers between devices  346 us (68%)
  local copies, waits for them, and re-layouts  53.5 us (11%)
  matrix products  41.3 us (8%)
  other arithmetic  41.1 us (8%)
  between operations  15.3 us (3%)
  starting transfers between devices  8.58 us (2%)
    all_gather x1, waiting for transfers between devices, gather_and_add(): blocks = lax.all_gather(value, axis, axis=0, tiled=False)  138 us
    reduce_scatter x1, waiting for transfers between devices, local(): lax.psum_scatter(lax.dot_general(columns, grad_out, (((0,), (0,)), ((), (...  89.4 us
    psum x1, waiting for transfers between devices, spread(): return lax.psum(jnp.where(mine, shard, jnp.zeros_like(shard)), axis)  88.4 us
    all_gather x1, waiting for transfers between devices, local(): lax.all_gather(out_weight, 'seq', axis=0, tiled=True)  29.6 us
    reduce_sum x1, other arithmetic, gather_and_add(): total = blocks.sum(axis=0)  12.1 us
  transfers between devices with their start and end apart: 8, of which 4 were waited for; matrix products, arithmetic and copies ran while one was open for 17% of the time, Pallas kernels for 0%

profile of v1, /device:TPU:0, one launch (start us, length us, event | category | flops | bytes accessed | tf_op | source)
XLA Modules:
  0.0 505.5 jit_solution(15254236575942950469)
XLA Ops:
  7.2 0.0 all-reduce.3.cloned.1.call-start
  7.2 1.3 fusion.34
  9.8 2.1 select_bitcast_fusion.1
  11.9 0.0 all-reduce.3.cloned.1.call-update
  12.0 0.0 all-gather.3.cloned.1.call-start
  12.0 0.7 all-gather.3.cloned.1.call-update
  12.7 0.0 all-gather.5.cloned.1.call-start
  12.8 1.3 collective-permute-start.1
  14.1 3.1 collective-permute-start
  17.1 0.7 fusion.53
  17.8 0.7 fusion.28
  18.5 0.7 fusion.52
  19.2 0.7 and_bitcast_fusion
  19.9 0.1 compare_and_fusion
  20.0 0.1 fusion.25
  20.0 0.1 broadcast_bitcast_fusion
  20.1 1.2 pad_maximum_fusion.2
  21.3 2.5 gather_fusion
  23.8 88.4 %all-reduce.3.cloned.1.call-done = (bf16[1,2,128,1024]{3,2,1,0:T(8,128)(2,1)}, bf16[1,2,128,1024]{3,2,1,0:T(8,128)(2,1)}) async-done(((bf16[1,2,128,1024]{3,2,1,0:T(8,128)(2,1)}, bf16[1,2,128,1024]{3,2,1,0:T(8,128)(2,1)}), (bf16[1,2,128,1024]{3,2,1,0:T(8,128)(2,1)}, bf16[1,2,128,1024]{3,2,1,0:T(8,128)(2,1)})) %all-reduce.3.cloned.1.call-update) | async-done | bytes 1048592 | tf_op jit(solution)/shard_map/psum | solution.py:33
  112.2 1.3 maximum_bitcast_fusion.2
  113.5 2.3 bitcast_select_fusion
  115.8 1.6 pad_maximum_fusion.1
  117.3 2.0 copy.76
  119.3 3.3 copy.52
  122.6 3.6 copy.75
  126.2 4.1 copy.70
  130.3 0.8 fusion.19
  131.1 3.5 fusion.35
  134.6 29.6 %all-gather.3.cloned.1.call-done = bf16[1024,2048]{1,0:T(8,128)(2,1)} async-done(((bf16[64,2048]{1,0:T(8,128)(2,1)}), bf16[1024,2048]{1,0:T(8,128)(2,1)}) %all-gather.3.cloned.1.call-update) | async-done | bytes 4194320 | tf_op jit(solution)/shard_map/all_gather | solution.py:148
  164.3 3.7 convolution_convert_fusion.3
  168.0 0.2 copy.73
  168.2 5.0 convolution_bitcast_fusion.1
  173.2 3.1 multiply_reduce_fusion
  176.3 5.4 %copy.58 = f32[1,1024,8,128]{3,2,1,0:T(8,128)} copy(f32[1,1024,8,128]{1,3,2,0:T(8,128)} %convolution_bitcast_fusion.1) | data formatting | bytes 8388608 | tf_op jit(solution)/shard_map/qhij,qihd->qjhd/transpose | solution.py:88
  181.7 4.9 stack.34
  186.6 4.2 multiply_convert_fusion
  190.8 1.3 copy-done.1
  192.1 0.7 convolution_bitcast_fusion.2
  192.8 4.4 copy.55
  197.2 5.0 stack.33
  202.2 5.7 %pad_maximum_fusion = f32[2,1,2,131072]{3,2,0,1:T(2,128)} fusion(f32[1,1,8,131072]{3,2,0,1:T(8,128)} %bitcast.140, f32[1,1,8,131072]{3,2,0,1:T(8,128)} %bitcast.142), kind=kLoop, calls=%fused_computation.22 | loop fusion | flops 524288 | bytes 10485760 | tf_op jit(solution)/shard_map/stack | solution.py:106
  207.9 4.1 all_gather_reshape.3
  211.9 0.0 all-gather.5.cloned.1.call-update
  212.0 0.3 reduce-scatter.2.cloned.1.call-start
  212.2 3.5 convolution_convert_fusion.2
  215.8 4.6 fusion.36
  220.4 0.6 copy-done.7
  221.1 0.1 add_bitcast_fusion
  221.2 2.3 convolution_convert_fusion.1
  223.4 0.9 copy.61
  224.3 9.9 %convolution_bitcast_fusion = f32[2,3,131072]{2,1,0:T(4,128)} fusion(f32[1,1,8,131072]{3,2,0,1:T(8,128)} %bitcast.141, f32[1,1,8,131072]{3,2,0,1:T(8,128)} %bitcast.143, s32[6]{0:T(128)S(1)} %add_bitcast_fusion), kind=kOutput, calls=%fused_computation.2 | convolution fusion | flops 58195984 | bytes 11534360 | tf_op jit(solution)/shard_map/sj,ksx->kjx/dot_general | solution.py:116
  234.2 5.1 %reshape.359 = f32[2,384,1024]{2,1,0:T(8,128)} reshape(f32[2,3,131072]{2,1,0:T(4,128)} %convolution_bitcast_fusion) | data formatting | bytes 6291456 | tf_op jit(solution)/shard_map/reshape | solution.py:117
  239.3 2.3 convert.6
  241.6 1.1 fusion.33
  242.7 2.3 collective-permute-start.2
  245.0 1.6 collective-permute-start.3
  246.5 1.5 convolution_convert_fusion
  248.1 137.6 %all-gather.5.cloned.1.call-done = f32[16,2,2,128,1024]{4,3,2,1,0:T(8,128)} async-done(((f32[1,2,2,128,1024]{4,3,2,1,0:T(8,128)}), f32[16,2,2,128,1024]{4,3,2,1,0:T(8,128)}) %all-gather.5.cloned.1.call-update) | async-done | bytes 33554448 | tf_op jit(solution)/shard_map/all_gather | solution.py:13
  385.7 12.1 %reduce_sum.33 = f32[2,2,128,1024]{3,2,1,0:T(8,128)S(1)} reduce(f32[16,2,2,128,1024]{4,3,2,1,0:T(8,128)} %all-gather.5.cloned.1.call-done, f32[]{:T(128)} %constant.59.clone.1), dimensions={0}, to_apply=%region_5.6 | reduce | flops 7864320 | bytes 35651588 | tf_op jit(solution)/shard_map/reduce_sum | solution.py:14
  397.8 2.8 reshape.360
  400.7 6.1 %fusion.26 = f32[1,2,128,1024]{3,0,2,1:T(1,128)S(1)} fusion(f32[2,128,1024,2]{2,3,1,0:T(2,128)} %bitcast.149, s32[2]{0:T(128)S(1)} %copy-done.6, s32[]{:T(128)S(6)} %axis_index.8), kind=kOutput, calls=%fused_computation.61 | convolution fusion | flops 6291458 | bytes 3145740 | tf_op jit(solution)/shard_map/gj,kgx->kjx/dot_general | solution.py:185
  406.7 2.0 fusion.15
  408.8 0.8 slice_bitcast_fusion
  409.6 89.4 %reduce-scatter.2.cloned.1.call-done = f32[64,2048]{1,0:T(8,128)} async-done(((f32[1024,2048]{1,0:T(8,128)}), f32[64,2048]{1,0:T(8,128)}) %reduce-scatter.2.cloned.1.call-update) | async-done | bytes 524304 | tf_op jit(solution)/shard_map/reduce_scatter | solution.py:162
  (26 shorter events, 0.1 us)
Async XLA Ops:
  7.2 157.1 %copy-start = (bf16[128,2048]{1,0:T(8,128)(2,1)S(1)}, bf16[128,2048]{1,0:T(8,128)(2,1)}, u32[]{:S(2)}) copy-start(bf16[128,2048]{1,0:T(8,128)(2,1)} %param.12) | copy-start | bytes 1572868
  7.2 105.0 %all-reduce.3.cloned.1.call-start = ((), (), s32[]{:S(2)}) async-start(), calls=%async_computation.4 | async-start | bytes 2097152 | tf_op jit(solution)/shard_map/psum | solution.py:33
  12.0 152.3 %all-gather.3.cloned.1.call-start = ((), (), s32[]{:S(2)}) async-start(), calls=%async_computation.1 | async-start | bytes 4456448 | tf_op jit(solution)/shard_map/all_gather | solution.py:148
  12.7 372.9 %all-gather.5.cloned.1.call-start = ((), (), s32[]{:S(2)}) async-start(), calls=%async_computation.2 | async-start | bytes 35651584 | tf_op jit(solution)/shard_map/all_gather | solution.py:13
  12.8 7.3 %collective-permute-start.1 = (bf16[2,128,1024]{2,1,0:T(8,128)(2,1)S(1)}, bf16[2,128,1024]{2,1,0:T(8,128)(2,1)S(1)}, u32[]{:S(2)}, u32[]{:S(2)}) collective-permute-start(bf16[2,128,1024]{2,1,0:T(8,128)(2,1)S(1)} %get-tuple-element.30), channel_id=1, source_target_pairs={{1,0},{2,1},{3,2},{4,3},{5,4},{6,5},{7,6},{8,7},{9,8},{10,9},{11,1... | collective-permute-start | bytes 1572872 | tf_op jit(solution)/shard_map/ppermute | solution.py:26
  14.1 6.0 %collective-permute-start = (bf16[2,128,1024]{2,1,0:T(8,128)(2,1)S(1)}, bf16[2,128,1024]{2,1,0:T(8,128)(2,1)S(1)}, u32[]{:S(2)}, u32[]{:S(2)}) collective-permute-start(bf16[2,128,1024]{2,1,0:T(8,128)(2,1)S(1)} %get-tuple-element.30), channel_id=1, source_target_pairs={{0,1},{1,2},{2,3},{3,4},{4,5},{5,6},{6,7},{7,8},{8,9},{9,10},{10,1... | collective-permute-start | bytes 1572872 | tf_op jit(solution)/shard_map/ppermute | solution.py:25
  122.6 7.8 %copy-start.5 = (bf16[128,1024]{1,0:T(8,128)(2,1)S(1)}, bf16[128,1024]{1,0:T(8,128)(2,1)}, u32[]{:S(2)}) copy-start(bf16[128,1024]{1,0:T(8,128)(2,1)} %param.8) | copy-start | bytes 786436
  168.2 5.1 %copy-start.3 = (f32[8,128,1024]{1,2,0:T(8,128)S(1)}, f32[8,128,1024]{1,2,0:T(8,128)}, u32[]{:S(2)}) copy-start(f32[8,128,1024]{1,2,0:T(8,128)} %get-tuple-element.34) | copy-start | bytes 12582916
  168.2 5.1 copy-start.4
  190.7 1.4 copy-start.1
  212.0 287.0 %reduce-scatter.2.cloned.1.call-start = ((), (), s32[]{:S(2)}) async-start(), calls=%async_computation.3 | async-start | bytes 8912896 | tf_op jit(solution)/shard_map/reduce_scatter | solution.py:162
  220.4 0.7 copy-start.7
  220.4 0.7 copy-start.8
  239.3 7.2 %copy-start.2 = (bf16[1024,2048]{1,0:T(8,128)(2,1)S(1)}, bf16[1024,2048]{1,0:T(8,128)(2,1)}, u32[]{:S(2)}) copy-start(bf16[1024,2048]{1,0:T(8,128)(2,1)} %all-gather.3.cloned.1.call-done) | copy-start | bytes 12582916
  242.7 164.1 %collective-permute-start.2 = (bf16[2,128,1024]{2,1,0:T(8,128)(2,1)}, bf16[2,128,1024]{2,1,0:T(8,128)(2,1)S(1)}, u32[]{:S(2)}, u32[]{:S(2)}) collective-permute-start(bf16[2,128,1024]{2,1,0:T(8,128)(2,1)} %get-tuple-element.24), channel_id=1, source_target_pairs={{0,1},{1,2},{2,3},{3,4},{4,5},{5,6},{6,7},{7,8},{8,9},{9,10},{10,1... | collective-permute-start | bytes 1572872 | tf_op jit(solution)/shard_map/ppermute | solution.py:25
  245.0 161.8 %collective-permute-start.3 = (bf16[2,128,1024]{2,1,0:T(8,128)(2,1)}, bf16[2,128,1024]{2,1,0:T(8,128)(2,1)}, u32[]{:S(2)}, u32[]{:S(2)}) collective-permute-start(bf16[2,128,1024]{2,1,0:T(8,128)(2,1)} %get-tuple-element.25), channel_id=1, source_target_pairs={{1,0},{2,1},{3,2},{4,3},{5,4},{6,5},{7,6},{8,7},{9,8},{10,9},{11,1... | collective-permute-start | bytes 1572872 | tf_op jit(solution)/shard_map/ppermute | solution.py:26
  397.8 2.9 copy-start.6
Sparse Core Ops, SparseCore 0:
  12.1 100.0 all-reduce.2
  114.4 49.8 all-gather.2
  212.1 173.5 all-gather.4
  390.1 108.8 reduce-scatter.1
